TPU v7x, 32 devices: a whole 2x2x4 slice. The times are simulated.
32 devices in a mesh: lat: 8 (over y, x, core), lon: 4 (over z).
Axes of the slice: x: 2, y: 2, z: 4, core: 2. Of those that a mesh axis runs over, the one named last changes fastest.
Arguments:
- tracers: float32 [5, 4, 64, 2880], P(None, None, 'lat', 'lon'), may hold values from -6 to 6
- courant_x: float32 [4, 64, 2880], P(None, 'lat', 'lon'), may hold values from -0.3 to 0.3
- courant_y: float32 [4, 64, 2880], P(None, 'lat', 'lon'), may hold values from -0.3 to 0.3
- cutoffs: int32 [64], replicated, may hold values from 1 to 720, as said below
Outputs:
- advected: float32 [5, 4, 64, 2880], P(None, None, 'lat', 'lon')
Inputs may be any that keep to these rules, and one draw needn't show every extreme that they name: `cutoffs`: some row poleward of 45 degrees keeps exactly 720 wavenumbers.
All inputs are finite; a program needn't handle non-finite values.
Results may differ from a plain program's by a relative error of at most 0.0003.
Values sent between devices are 32-bit elements; how exact they have to be, the bound alone decides.
No kernel may reach another device: no remote copies, remote signals or barrier semaphores. Data moves between devices by JAX's collectives and lax.ppermute only.
A program may use at most 64 MiB of HBM per device.

v0:
```python
import math
import jax
import jax.numpy as jnp
from jax import lax
from jax.sharding import PartitionSpec as P

KMAX = 720
SUBSTEPS = 2


def extended_2(cells, sides, width):
    for axis, dim in sides:
        count = lax.axis_size(axis)
        head = lax.slice_in_dim(cells, 0, width, axis=dim)
        tail = lax.slice_in_dim(cells, cells.shape[dim] - width, cells.shape[dim], axis=dim)
        cells = jnp.concatenate(
            [
                lax.ppermute(tail, axis, [(i, (i + 1) % count) for i in range(count)]),
                cells,
                lax.ppermute(head, axis, [((i + 1) % count, i) for i in range(count)]),
            ],
            axis=dim,
        )
    return cells


def from_behind(x, axis, by):
    size = lax.axis_size(axis)
    return lax.ppermute(x, axis, [(i, (i + by) % size) for i in range(size)])


def window(values, first_cell, last_cell, dim_at):
    return lax.slice_in_dim(values, first_cell, last_cell, axis=dim_at)


def ppm_flux(padded, courant, dim_at, cell_count):
    edge_values = 7.0 / 12.0 * (
        window(padded, 1, cell_count + 4, dim_at) + window(padded, 2, cell_count + 5, dim_at)
    ) - 1.0 / 12.0 * (
        window(padded, 0, cell_count + 3, dim_at) + window(padded, 3, cell_count + 6, dim_at)
    )
    left_edge = window(edge_values, 0, cell_count + 1, dim_at)
    mid_edge = window(edge_values, 1, cell_count + 2, dim_at)
    right_edge = window(edge_values, 2, cell_count + 3, dim_at)
    left_cell = window(padded, 2, cell_count + 3, dim_at)
    right_cell = window(padded, 3, cell_count + 4, dim_at)
    magnitude = jnp.abs(courant)
    six_left = 6.0 * left_cell - 3.0 * (left_edge + mid_edge)
    six_right = 6.0 * right_cell - 3.0 * (mid_edge + right_edge)
    from_left = mid_edge - 0.5 * magnitude * (
        mid_edge - left_edge - (1.0 - magnitude * (2.0 / 3.0)) * six_left
    )
    from_right = mid_edge + 0.5 * magnitude * (
        right_edge - mid_edge + (1.0 - magnitude * (2.0 / 3.0)) * six_right
    )
    return courant * jnp.where(courant >= 0.0, from_left, from_right)


def dft_basis(first_col, column_count, circle):
    position = first_col + jnp.arange(column_count, dtype=jnp.int32)
    wavenumber = jnp.arange(KMAX, dtype=jnp.int32)
    phase_index = position[:, None] * wavenumber[None, :] % circle
    phase_angle = phase_index.astype(jnp.float32) * (2.0 * math.pi / circle)
    return jnp.concatenate([jnp.cos(phase_angle), jnp.sin(phase_angle)], axis=1)


def mode_weights(cut_rows, circle):
    wavenumber = jnp.arange(KMAX, dtype=jnp.int32)
    mode_scale = jnp.where(wavenumber == 0, 1.0 / circle, 2.0 / circle).astype(jnp.float32)
    weights = jnp.where(wavenumber[None, :] < cut_rows[:, None], mode_scale[None, :], 0.0)
    return jnp.concatenate([weights, weights], axis=1)


def on_device(tracers, courant_x, courant_y, cutoffs):
    tracer_count, level_count, lat_rows, lon_cols = tracers.shape
    field_count = tracer_count * level_count
    lat_devices = lax.axis_size("lat")
    lon_devices = lax.axis_size("lon")
    lat_index = lax.axis_index("lat")
    lon_index = lax.axis_index("lon")
    circle = lon_cols * lon_devices
    total_rows = lat_rows * lat_devices
    row_global = lat_index * lat_rows + jnp.arange(lat_rows, dtype=jnp.int32)
    face_global = lat_index * lat_rows + jnp.arange(lat_rows + 1, dtype=jnp.int32)
    face_angle = (face_global.astype(jnp.float32) / total_rows - 0.5) * math.pi
    face_weight = jnp.where(
        (face_global == 0) | (face_global == total_rows), 0.0, jnp.cos(face_angle)
    )
    center_weight = jnp.cos(((row_global.astype(jnp.float32) + 0.5) / total_rows - 0.5) * math.pi)
    polar_rows = (row_global < total_rows // 4) | (row_global >= total_rows - total_rows // 4)
    basis_tile = dft_basis(lon_index * lon_cols, lon_cols, circle)
    state = tracers
    for substep in range(SUBSTEPS):
        flat_rows = state.reshape(field_count, lat_rows, lon_cols)
        stacked = jnp.concatenate([flat_rows, courant_x, courant_y], axis=0)
        padded = extended_2(stacked, (("lat", 1), ("lon", 2)), 3)
        pad_tracer = padded[:field_count].reshape(
            tracer_count, level_count, lat_rows + 6, lon_cols + 6
        )
        pad_east = padded[field_count : field_count + level_count]
        pad_north = padded[field_count + level_count :]
        east_courant = pad_east[:, 3 : 3 + lat_rows, 2 : lon_cols + 3]
        zonal = ppm_flux(pad_tracer[:, :, 3 : 3 + lat_rows, :], east_courant, 3, lon_cols)
        edge_rows = jnp.concatenate([state[:, :, :3], state[:, :, lat_rows - 3 :]], axis=2)
        antipodal = from_behind(edge_rows, "lon", lon_devices // 2)
        south_rows = jnp.where(
            lat_index == 0, antipodal[:, :, 2::-1], pad_tracer[:, :, :3, 3 : 3 + lon_cols]
        )
        north_rows = jnp.where(
            lat_index == lat_devices - 1,
            antipodal[:, :, 5:2:-1],
            pad_tracer[:, :, lat_rows + 3 :, 3 : 3 + lon_cols],
        )
        extended = jnp.concatenate(
            [south_rows, pad_tracer[:, :, 3 : 3 + lat_rows, 3 : 3 + lon_cols], north_rows], axis=2
        )
        north_courant = pad_north[:, 3 : lat_rows + 4, 3 : 3 + lon_cols]
        meridional = ppm_flux(extended, north_courant, 2, lat_rows) * face_weight[:, None]
        change = (
            zonal[..., 1:]
            - zonal[..., :-1]
            + (meridional[:, :, 1:] - meridional[:, :, :-1]) / center_weight[:, None]
        )
        state = state - change
        flat_rows = state.reshape(field_count * lat_rows, lon_cols)
        band_cuts = lax.dynamic_slice_in_dim(cutoffs, lat_index * lat_rows, lat_rows)
        cut_rows = jnp.tile(band_cuts, field_count)
        partial_value = jnp.dot(flat_rows, basis_tile, precision=lax.Precision.HIGHEST)
        spectra = lax.psum(partial_value, "lon")
        weighted = spectra * mode_weights(cut_rows, circle)
        smooth = jnp.dot(weighted, basis_tile.T, precision=lax.Precision.HIGHEST)
        polar_flat = jnp.tile(polar_rows, field_count)
        filtered_rows = jnp.where(polar_flat[:, None], smooth, flat_rows)
        state = filtered_rows.reshape(tracer_count, level_count, lat_rows, lon_cols)
    return state


def solution(mesh):
    in_specs = (P(None, None, "lat", "lon"), P(None, "lat", "lon"), P(None, "lat", "lon"), P())
    out_specs = P(None, None, "lat", "lon")
    return jax.shard_map(
        on_device, mesh=mesh, in_specs=in_specs, out_specs=out_specs, check_vma=False
    )
```

profile of v0, /device:TPU:0, one launch (start us, length us, event | category | flops | bytes accessed | tf_op | source)
XLA Modules:
  0.0 247.9 jit_solution(7881026659669633347)
XLA Ops:
  6.5 1.3 fusion.126
  7.9 0.9 pad_maximum_fusion.28
  8.8 4.1 %collective-permute-start.4 = (f32[5,4,6,720]{3,2,1,0:T(8,128)}, f32[5,4,6,720]{3,2,1,0:T(8,128)}, u32[]{:S(2)}, u32[]{:S(2)}) collective-permute-start(f32[5,4,6,720]{3,2,1,0:T(8,128)} %pad_maximum_fusion.28), channel_id=1, source_target_pairs={{0,2},{1,3},{2,0},{3,1},{4,6},{5,7},{6,4},{7,5},{8,10},{9,11},{10,... | collective-permute-start | bytes 1036808 | tf_op jit(solution)/shard_map/ppermute | solution.py:29
  12.8 1.0 pad_maximum_fusion.25
  13.8 0.9 fusion.122
  14.8 2.6 %collective-permute-start.1 = (f32[28,3,720]{2,1,0:T(4,128)}, f32[28,3,720]{2,1,0:T(4,128)S(1)}, u32[]{:S(2)}, u32[]{:S(2)}) collective-permute-start(f32[28,3,720]{2,1,0:T(4,128)} %get-tuple-element.24), channel_id=1, source_target_pairs={{4,0},{8,4},{12,8},{16,12},{20,16},{24,20},{28,24},{0,28},{5,1},{9... | collective-permute-start | bytes 725768 | tf_op jit(solution)/shard_map/ppermute | solution.py:20
  17.6 10.8 %fusion.5 = (f32[720,720]{1,0:T(8,128)S(1)}, f32[720,720]{1,0:T(8,128)}) fusion(s32[720]{0:T(1024)S(1)} %iota_add_fusion), kind=kLoop, calls=%fused_computation.8 | loop fusion | flops 4665600 | bytes 4150080 | tf_op jit(solution)/shard_map/cos | solution.py:64
  28.4 1.4 fusion.12
  29.8 0.1 fusion.120
  29.9 1.6 collective-permute-start.2
  31.5 2.2 collective-permute-start.3
  33.8 0.8 abs_multiply_fusion.1
  34.6 5.6 %collective-permute-done.2 = f32[28,14,3]{2,1,0:T(8,128)S(1)} collective-permute-done((f32[28,14,3]{2,1,0:T(8,128)S(1)}, f32[28,14,3]{2,1,0:T(8,128)S(1)}, u32[]{:S(2)}, u32[]{:S(2)}) %collective-permute-start.2) | collective-permute-done | bytes 4736 | tf_op jit(solution)/shard_map/ppermute | solution.py:18
  40.2 4.4 %collective-permute-done.3 = f32[28,14,3]{2,1,0:T(8,128)S(1)} collective-permute-done((f32[28,14,3]{2,1,0:T(8,128)S(1)}, f32[28,14,3]{2,1,0:T(8,128)S(1)}, u32[]{:S(2)}, u32[]{:S(2)}) %collective-permute-start.3) | collective-permute-done | bytes 4736 | tf_op jit(solution)/shard_map/ppermute | solution.py:20
  44.6 1.7 fusion.60
  46.4 0.4 fusion.105
  46.8 0.9 broadcast_compare_fusion.3
  47.8 1.0 slice.329
  48.8 1.4 fusion.98
  50.2 2.1 fusion.125
  52.2 3.7 %rev.12 = f32[5,4,3,720]{3,2,1,0:T(4,128)} reverse(f32[5,4,3,720]{3,2,1,0:T(4,128)} %get-tuple-element.29), dimensions={2} | reverse | bytes 345600 | tf_op jit(solution)/shard_map/rev | solution.py:107
  56.0 3.7 %rev.13 = f32[5,4,3,720]{3,2,1,0:T(4,128)} reverse(f32[5,4,3,720]{3,2,1,0:T(4,128)} %get-tuple-element.30), dimensions={2} | reverse | bytes 345600 | tf_op jit(solution)/shard_map/rev | solution.py:111
  59.7 1.3 slice_select_fusion.3
  61.0 1.2 pad_maximum_fusion.21
  62.3 0.4 fusion.56
  62.7 0.5 copy-done.18
  63.4 1.0 fusion.43
  64.4 0.1 copy-done.13
  64.5 0.2 fusion.91
  64.8 1.4 copy-done
  66.2 4.2 %fusion.10 = f32[160,1440]{1,0:T(8,128)} fusion(f32[160,720]{1,0:T(8,128)S(1)} %bitcast.30, f32[720,720]{1,0:T(8,128)S(1)} %copy-done, f32[720,720]{1,0:T(8,128)S(1)} %get-tuple-element.41), kind=kOutput, calls=%fused_computation.13 | convolution fusion | flops 1991692800 | bytes 5529600 | tf_op jit(solution)/shard_map/dot_general | solution.py:128
  70.4 0.2 all-reduce.5.cloned.1.call-start
  71.0 0.9 fusion.107
  71.8 49.4 %all-reduce.3.cloned.1.call-done = f32[160,1440]{1,0:T(8,128)} async-done(((f32[160,1440]{1,0:T(8,128)}), f32[160,1440]{1,0:T(8,128)}) %all-reduce.3.cloned.1.call-update) | async-done | bytes 921616 | tf_op jit(solution)/shard_map/psum | solution.py:129
  121.3 6.8 %fusion.15 = f32[160,720]{1,0:T(8,128)S(1)} fusion(f32[160,720]{1,0:T(8,128)S(1)} %bitcast.31, f32[720,720]{1,0:T(8,128)} %get-tuple-element.42, f32[720,720]{1,0:T(8,128)S(1)} %get-tuple-element.41, f32[160,1440]{1,0:T(8,128)} %all-reduce.3.cloned.1.call-done, f32[160,720]{1,0:T(8,128)} %fusion.107, pred[160]{0:T(512)(128)(4,1)S(1)} %broadcast_in_dim.83), kind=kOutput, calls=%fused_computation.34 | convolution fusion | flops 1992268800 | bytes 6451360 | tf_op jit(solution)/shard_map/dot_general | solution.py:131
  128.3 2.6 %collective-permute-start.6 = (f32[28,3,720]{2,1,0:T(4,128)S(1)}, f32[28,3,720]{2,1,0:T(4,128)S(1)}, u32[]{:S(2)}, u32[]{:S(2)}) collective-permute-start(f32[28,3,720]{2,1,0:T(4,128)S(1)} %get-tuple-element.22), channel_id=1, source_target_pairs={{4,0},{8,4},{12,8},{16,12},{20,16},{24,20},{28,24},{0,28},{5,1},{9... | collective-permute-start | bytes 725768 | tf_op jit(solution)/shard_map/ppermute | solution.py:20
  131.0 0.1 pad_maximum_fusion.29
  131.1 1.7 collective-permute-start.9
  132.8 5.0 %collective-permute-done.5 = f32[28,3,720]{2,1,0:T(4,128)S(1)} collective-permute-done((f32[28,3,720]{2,1,0:T(4,128)S(1)}, f32[28,3,720]{2,1,0:T(4,128)S(1)}, u32[]{:S(2)}, u32[]{:S(2)}) %collective-permute-start.5) | collective-permute-done | bytes 241952 | tf_op jit(solution)/shard_map/ppermute | solution.py:18
  137.8 0.3 fusion.14
  138.1 0.1 fusion.119
  138.2 1.3 collective-permute-start.7
  139.5 2.5 %collective-permute-start.8 = (f32[28,14,3]{2,1,0:T(8,128)S(1)}, f32[28,14,3]{2,1,0:T(8,128)S(1)}, u32[]{:S(2)}, u32[]{:S(2)}) collective-permute-start(f32[28,14,3]{2,1,0:T(8,128)S(1)} %get-tuple-element.14), channel_id=1, source_target_pairs={{1,0},{2,1},{3,2},{0,3},{5,4},{6,5},{7,6},{4,7},{9,8},{10,9},{11,1... | collective-permute-start | bytes 14120 | tf_op jit(solution)/shard_map/ppermute | solution.py:20
  142.1 0.8 abs_multiply_fusion
  142.9 7.7 %collective-permute-done.7 = f32[28,14,3]{2,1,0:T(8,128)S(1)} collective-permute-done((f32[28,14,3]{2,1,0:T(8,128)S(1)}, f32[28,14,3]{2,1,0:T(8,128)S(1)}, u32[]{:S(2)}, u32[]{:S(2)}) %collective-permute-start.7) | collective-permute-done | bytes 4736 | tf_op jit(solution)/shard_map/ppermute | solution.py:18
  150.7 11.3 %collective-permute-done.8 = f32[28,14,3]{2,1,0:T(8,128)S(1)} collective-permute-done((f32[28,14,3]{2,1,0:T(8,128)S(1)}, f32[28,14,3]{2,1,0:T(8,128)S(1)}, u32[]{:S(2)}, u32[]{:S(2)}) %collective-permute-start.8) | collective-permute-done | bytes 4736 | tf_op jit(solution)/shard_map/ppermute | solution.py:20
  162.0 0.7 fusion.64
  162.6 0.4 fusion.87
  163.1 0.1 broadcast_compare_fusion.2
  163.2 1.0 slice.362
  164.2 1.4 fusion.80
  165.6 0.9 fusion.123
  166.5 3.8 %rev.14 = f32[5,4,3,720]{3,2,1,0:T(4,128)} reverse(f32[5,4,3,720]{3,2,1,0:T(4,128)} %get-tuple-element.25), dimensions={2} | reverse | bytes 345600 | tf_op jit(solution)/shard_map/rev | solution.py:107
  170.2 3.8 %rev.15 = f32[5,4,3,720]{3,2,1,0:T(4,128)} reverse(f32[5,4,3,720]{3,2,1,0:T(4,128)} %get-tuple-element.26), dimensions={2} | reverse | bytes 345600 | tf_op jit(solution)/shard_map/rev | solution.py:111
  174.0 1.6 slice_select_fusion.1
  175.6 0.2 pad_maximum_fusion.23
  175.9 0.4 fusion.53
  176.3 0.5 copy-done.16
  177.0 1.0 fusion.26
  178.0 0.2 fusion.73
  178.2 1.4 copy-done.1
  179.6 4.2 %fusion.8 = f32[160,1440]{1,0:T(8,128)} fusion(f32[160,720]{1,0:T(8,128)S(1)} %bitcast.32, f32[720,720]{1,0:T(8,128)S(1)} %copy-done.1, f32[720,720]{1,0:T(8,128)S(1)} %get-tuple-element.41), kind=kOutput, calls=%fused_computation.11 | convolution fusion | flops 1991692800 | bytes 5529600 | tf_op jit(solution)/shard_map/dot_general | solution.py:128
  183.8 49.9 %all-reduce.5.cloned.1.call-done = f32[160,1440]{1,0:T(8,128)} async-done(((f32[160,1440]{1,0:T(8,128)}), f32[160,1440]{1,0:T(8,128)}) %all-reduce.5.cloned.1.call-update) | async-done | bytes 921616 | tf_op jit(solution)/shard_map/psum | solution.py:129
  233.7 7.3 %fusion.16 = f32[160,720]{1,0:T(8,128)} fusion(f32[160,720]{1,0:T(8,128)S(1)} %bitcast.33, f32[720,720]{1,0:T(8,128)} %get-tuple-element.42, f32[720,720]{1,0:T(8,128)S(1)} %get-tuple-element.41, f32[160,1440]{1,0:T(8,128)} %all-reduce.5.cloned.1.call-done, f32[160,720]{1,0:T(8,128)S(1)} %copy-done.14, pred[160]{0:T(512)(128)(4,1)S(1)} %broadcast_in_dim.83), kind=kOutput, calls=%fused_computation.35 | convolution fusion | flops 1992268800 | bytes 6451360 | tf_op jit(solution)/shard_map/dot_general | solution.py:131
  (70 shorter events, 1.4 us)
Async XLA Ops:
  6.5 6.3 %copy-start.3 = (f32[5,4,8,720]{3,2,1,0:T(8,128)S(1)}, f32[5,4,8,720]{3,2,1,0:T(8,128)}, u32[]{:S(2)}) copy-start(f32[5,4,8,720]{3,2,1,0:T(8,128)} %param.4) | copy-start | bytes 1382404
  6.5 114.7 %all-reduce.3.cloned.1.call-start = ((), (), s32[]{:S(2)}) async-start(), calls=%async_computation | async-start | bytes 1966080 | tf_op jit(solution)/shard_map/psum | solution.py:129
  8.8 41.4 %collective-permute-start.4 = (f32[5,4,6,720]{3,2,1,0:T(8,128)}, f32[5,4,6,720]{3,2,1,0:T(8,128)}, u32[]{:S(2)}, u32[]{:S(2)}) collective-permute-start(f32[5,4,6,720]{3,2,1,0:T(8,128)} %pad_maximum_fusion.28), channel_id=1, source_target_pairs={{0,2},{1,3},{2,0},{3,1},{4,6},{5,7},{6,4},{7,5},{8,10},{9,11},{10,... | collective-permute-start | bytes 1036808 | tf_op jit(solution)/shard_map/ppermute | solution.py:29
  14.8 13.5 %collective-permute-start = (f32[28,3,720]{2,1,0:T(4,128)}, f32[28,3,720]{2,1,0:T(4,128)}, u32[]{:S(2)}, u32[]{:S(2)}) collective-permute-start(f32[28,3,720]{2,1,0:T(4,128)} %get-tuple-element.23), channel_id=1, source_target_pairs={{0,4},{4,8},{8,12},{12,16},{16,20},{20,24},{24,28},{28,0},{1,5},{5... | collective-permute-start | bytes 725768 | tf_op jit(solution)/shard_map/ppermute | solution.py:18
  14.8 13.5 %collective-permute-start.1 = (f32[28,3,720]{2,1,0:T(4,128)}, f32[28,3,720]{2,1,0:T(4,128)S(1)}, u32[]{:S(2)}, u32[]{:S(2)}) collective-permute-start(f32[28,3,720]{2,1,0:T(4,128)} %get-tuple-element.24), channel_id=1, source_target_pairs={{4,0},{8,4},{12,8},{16,12},{20,16},{24,20},{28,24},{0,28},{5,1},{9... | collective-permute-start | bytes 725768 | tf_op jit(solution)/shard_map/ppermute | solution.py:20
  17.5 10.8 %copy-start.6 = (f32[4,8,720]{2,1,0:T(8,128)S(1)}, f32[4,8,720]{2,1,0:T(8,128)}, u32[]{:S(2)}) copy-start(f32[4,8,720]{2,1,0:T(8,128)} %param.6) | copy-start | bytes 276484
  17.6 10.8 %copy-start.7 = (f32[4,8,720]{2,1,0:T(8,128)S(1)}, f32[4,8,720]{2,1,0:T(8,128)}, u32[]{:S(2)}) copy-start(f32[4,8,720]{2,1,0:T(8,128)} %param.5) | copy-start | bytes 276484
  28.3 16.3 %copy-start.4 = (f32[5,4,8,720]{3,2,1,0:T(8,128)S(1)}, f32[5,4,8,720]{3,2,1,0:T(8,128)}, u32[]{:S(2)}) copy-start(f32[5,4,8,720]{3,2,1,0:T(8,128)} %param.4) | copy-start | bytes 1382404
  28.4 5.4 %copy-start.10 = (f32[28,3,720]{2,1,0:T(4,128)}, f32[28,3,720]{2,1,0:T(4,128)S(1)}, u32[]{:S(2)}) copy-start(f32[28,3,720]{2,1,0:T(4,128)S(1)} %collective-permute-done.1) | copy-start | bytes 725764
  29.9 10.4 %collective-permute-start.2 = (f32[28,14,3]{2,1,0:T(8,128)S(1)}, f32[28,14,3]{2,1,0:T(8,128)S(1)}, u32[]{:S(2)}, u32[]{:S(2)}) collective-permute-start(f32[28,14,3]{2,1,0:T(8,128)S(1)} %get-tuple-element.15), channel_id=1, source_target_pairs={{0,1},{1,2},{2,3},{3,0},{4,5},{5,6},{6,7},{7,4},{8,9},{9,10},{10,1... | collective-permute-start | bytes 14120 | tf_op jit(solution)/shard_map/ppermute | solution.py:18
  31.5 13.1 %collective-permute-start.3 = (f32[28,14,3]{2,1,0:T(8,128)S(1)}, f32[28,14,3]{2,1,0:T(8,128)S(1)}, u32[]{:S(2)}, u32[]{:S(2)}) collective-permute-start(f32[28,14,3]{2,1,0:T(8,128)S(1)} %get-tuple-element.16), channel_id=1, source_target_pairs={{1,0},{2,1},{3,2},{0,3},{5,4},{6,5},{7,6},{4,7},{9,8},{10,9},{11,1... | collective-permute-start | bytes 14120 | tf_op jit(solution)/shard_map/ppermute | solution.py:20
  33.8 6.4 %copy-start.17 = (f32[4,9,720]{2,1,0:T(8,128)}, f32[4,9,720]{2,1,0:T(8,128)S(1)}, u32[]{:S(2)}) copy-start(f32[4,9,720]{2,1,0:T(8,128)S(1)} %get-tuple-element.12) | copy-start | bytes 311044
  34.6 12.2 %copy-start.11 = (f32[28,3,720]{2,1,0:T(4,128)S(1)}, f32[28,3,720]{2,1,0:T(4,128)}, u32[]{:S(2)}) copy-start(f32[28,3,720]{2,1,0:T(4,128)} %copy-done.10) | copy-start | bytes 725764
  59.7 2.6 %copy-start.9 = (f32[5,4,8,720]{3,2,1,0:T(8,128)S(1)}, f32[5,4,8,720]{3,2,1,0:T(8,128)}, u32[]{:S(2)}) copy-start(f32[5,4,8,720]{3,2,1,0:T(8,128)} %slice.329) | copy-start | bytes 1382404
  62.2 0.9 copy-start.18
  62.3 1.0 copy-start.21
  62.3 1.1 copy-start.22
  63.4 1.0 copy-start.5
  63.4 1.2 copy-start.13
  64.5 1.6 copy-start
  66.2 4.6 %copy-start.23 = (s32[64]{0:T(128)S(1)}, s32[64]{0:T(128)}, u32[]{:S(2)}) copy-start(s32[64]{0:T(128)} %param.7) | copy-start | bytes 772
  70.4 163.3 %all-reduce.5.cloned.1.call-start = ((), (), s32[]{:S(2)}) async-start(), calls=%async_computation.1 | async-start | bytes 1966080 | tf_op jit(solution)/shard_map/psum | solution.py:129
  128.3 9.5 %collective-permute-start.5 = (f32[28,3,720]{2,1,0:T(4,128)S(1)}, f32[28,3,720]{2,1,0:T(4,128)S(1)}, u32[]{:S(2)}, u32[]{:S(2)}) collective-permute-start(f32[28,3,720]{2,1,0:T(4,128)S(1)} %get-tuple-element.21), channel_id=1, source_target_pairs={{0,4},{4,8},{8,12},{12,16},{16,20},{20,24},{24,28},{28,0},{1,5},{5... | collective-permute-start | bytes 725768 | tf_op jit(solution)/shard_map/ppermute | solution.py:18
  128.3 9.5 %collective-permute-start.6 = (f32[28,3,720]{2,1,0:T(4,128)S(1)}, f32[28,3,720]{2,1,0:T(4,128)S(1)}, u32[]{:S(2)}, u32[]{:S(2)}) collective-permute-start(f32[28,3,720]{2,1,0:T(4,128)S(1)} %get-tuple-element.22), channel_id=1, source_target_pairs={{4,0},{8,4},{12,8},{16,12},{20,16},{24,20},{28,24},{0,28},{5,1},{9... | collective-permute-start | bytes 725768 | tf_op jit(solution)/shard_map/ppermute | solution.py:20
  131.1 34.5 %collective-permute-start.9 = (f32[5,4,6,720]{3,2,1,0:T(8,128)S(1)}, f32[5,4,6,720]{3,2,1,0:T(8,128)S(1)}, u32[]{:S(2)}, u32[]{:S(2)}) collective-permute-start(f32[5,4,6,720]{3,2,1,0:T(8,128)S(1)} %pad_maximum_fusion.29), channel_id=1, source_target_pairs={{0,2},{1,3},{2,0},{3,1},{4,6},{5,7},{6,4},{7,5},{8,10},{9,11},{10,... | collective-permute-start | bytes 1036808 | tf_op jit(solution)/shard_map/ppermute | solution.py:29
  138.2 12.5 %collective-permute-start.7 = (f32[28,14,3]{2,1,0:T(8,128)S(1)}, f32[28,14,3]{2,1,0:T(8,128)S(1)}, u32[]{:S(2)}, u32[]{:S(2)}) collective-permute-start(f32[28,14,3]{2,1,0:T(8,128)S(1)} %get-tuple-element.13), channel_id=1, source_target_pairs={{0,1},{1,2},{2,3},{3,0},{4,5},{5,6},{6,7},{7,4},{8,9},{9,10},{10,1... | collective-permute-start | bytes 14120 | tf_op jit(solution)/shard_map/ppermute | solution.py:18
  139.5 22.4 %collective-permute-start.8 = (f32[28,14,3]{2,1,0:T(8,128)S(1)}, f32[28,14,3]{2,1,0:T(8,128)S(1)}, u32[]{:S(2)}, u32[]{:S(2)}) collective-permute-start(f32[28,14,3]{2,1,0:T(8,128)S(1)} %get-tuple-element.14), channel_id=1, source_target_pairs={{1,0},{2,1},{3,2},{0,3},{5,4},{6,5},{7,6},{4,7},{9,8},{10,9},{11,1... | collective-permute-start | bytes 14120 | tf_op jit(solution)/shard_map/ppermute | solution.py:20
  142.1 8.6 %copy-start.15 = (f32[4,9,720]{2,1,0:T(8,128)}, f32[4,9,720]{2,1,0:T(8,128)S(1)}, u32[]{:S(2)}) copy-start(f32[4,9,720]{2,1,0:T(8,128)S(1)} %get-tuple-element.8) | copy-start | bytes 311044
  162.6 1.6 copy-start.2
  165.6 10.0 %copy-start.8 = (f32[5,4,8,720]{3,2,1,0:T(8,128)S(1)}, f32[5,4,8,720]{3,2,1,0:T(8,128)}, u32[]{:S(2)}) copy-start(f32[5,4,8,720]{3,2,1,0:T(8,128)} %slice.362) | copy-start | bytes 1382404
  175.8 0.9 copy-start.16
  175.8 1.0 copy-start.19
  175.9 1.1 copy-start.20
  177.0 1.0 copy-start.12
  178.0 1.6 copy-start.1
  179.6 54.1 %copy-start.14 = (f32[160,720]{1,0:T(8,128)S(1)}, f32[160,720]{1,0:T(8,128)}, u32[]{:S(2)}) copy-start(f32[160,720]{1,0:T(8,128)} %fusion.107) | copy-start | bytes 1382404
Sparse Core Ops, SparseCore 0:
  70.5 50.6 all-reduce.2
  184.0 49.7 all-reduce.4
where the time goes:
time: 250 us; the launch traced here: 248 us
  waiting for transfers between devices  133 us (53%)
  other arithmetic  31.8 us (13%)
  local copies, waits for them, and re-layouts  27.3 us (11%)
  matrix products  22.5 us (9%)
  starting transfers between devices  19 us (8%)
  between operations  13.8 us (6%)
    psum x2, waiting for transfers between devices, on_device(): spectra = lax.psum(partial_value, 'lon')  99.3 us
    ppermute x4, waiting for transfers between devices, extended_2(): lax.ppermute(tail, axis, [(i, (i + 1) % count) for i in range(count)])  18.3 us
    ppermute x4, waiting for transfers between devices, extended_2(): lax.ppermute(head, axis, [((i + 1) % count, i) for i in range(count)])  15.7 us
    dot_general x2, matrix products, on_device(): smooth = jnp.dot(weighted, basis_tile.T, precision=lax.Precision.HIGHEST)  14.1 us
    cos x1, other arithmetic, dft_basis(): return jnp.concatenate([jnp.cos(phase_angle), jnp.sin(phase_angle)], axis=1)  10.8 us
    ppermute x4, starting transfers between devices, extended_2(): lax.ppermute(head, axis, [((i + 1) % count, i) for i in range(count)])  10.1 us
    dot_general x2, matrix products, on_device(): jnp.dot(flat_rows, basis_tile, precision=lax.Precision.HIGHEST)  8.42 us
    rev x2, local copies, waits for them, and re-layouts, on_device(): antipodal[:, :, 2::-1]  7.49 us
  transfers between devices with their start and end apart: 12, of which 7 were waited for; matrix products, arithmetic and copies ran while one was open for 11% of the time, Pallas kernels for 0%

commit v1 on v0

--- a/solution.py
+++ b/solution.py
@@ -126,7 +126,13 @@
         band_cuts = lax.dynamic_slice_in_dim(cutoffs, lat_index * lat_rows, lat_rows)
         cut_rows = jnp.tile(band_cuts, field_count)
         partial_value = jnp.dot(flat_rows, basis_tile, precision=lax.Precision.HIGHEST)
-        spectra = lax.psum(partial_value, "lon")
+        devices = lax.axis_size("lon")
+        spectra, far = (partial_value, 1)
+        while far < devices:
+            spectra = spectra + lax.ppermute(
+                spectra, "lon", [(i_2, i_2 ^ far) for i_2 in range(devices)]
+            )
+            far = 2 * far
         weighted = spectra * mode_weights(cut_rows, circle)
         smooth = jnp.dot(weighted, basis_tile.T, precision=lax.Precision.HIGHEST)
         polar_flat = jnp.tile(polar_rows, field_count)

time: 250 us -> 271 us (1.084)
  waiting for transfers between devices: 133 us -> 161 us
  between operations: 13.8 us -> 0.46 us
  starting transfers between devices: 19 us -> 28.4 us
  matrix products: 22.5 us -> 18.7 us
    ppermute x0 -> x4, waiting for transfers between devices: none -> 126 us  [on_device(): lax.ppermute(spectra, 'lon', [(i_2, i_2 ^ far) for i_2 in range(devices)])]
    psum x2 -> x0, waiting for transfers between devices: 99.3 us -> none  [on_device(): spectra = lax.psum(partial_value, 'lon')]
    ppermute x0 -> x4, starting transfers between devices: none -> 8.93 us  [on_device(): lax.ppermute(spectra, 'lon', [(i_2, i_2 ^ far) for i_2 in range(devices)])]
  transfers between devices with their start and end apart: 12 -> 14, of which waited for: 7 -> 10; matrix products, arithmetic and copies ran while one was open for 11% -> 10% of each run, Pallas kernels for 0% -> 0%
where the time goes in v1:
time: 271 us; the launch traced here: 268 us
  waiting for transfers between devices  161 us (59%)
  other arithmetic  32.2 us (12%)
  starting transfers between devices  28.4 us (10%)
  local copies, waits for them, and re-layouts  27.3 us (10%)
  matrix products  18.7 us (7%)
    ppermute x4, waiting for transfers between devices, on_device(): lax.ppermute(spectra, 'lon', [(i_2, i_2 ^ far) for i_2 in range(devices)])  126 us
    ppermute x4, waiting for transfers between devices, extended_2(): lax.ppermute(tail, axis, [(i, (i + 1) % count) for i in range(count)])  18.3 us
    ppermute x4, waiting for transfers between devices, extended_2(): lax.ppermute(head, axis, [((i + 1) % count, i) for i in range(count)])  16.4 us
    ppermute x4, starting transfers between devices, extended_2(): lax.ppermute(head, axis, [((i + 1) % count, i) for i in range(count)])  12.2 us
    dot_general x2, matrix products, on_device(): smooth = jnp.dot(weighted, basis_tile.T, precision=lax.Precision.HIGHEST)  12.2 us
    cos x1, other arithmetic, dft_basis(): return jnp.concatenate([jnp.cos(phase_angle), jnp.sin(phase_angle)], axis=1)  10.8 us
    ppermute x4, starting transfers between devices, on_device(): lax.ppermute(spectra, 'lon', [(i_2, i_2 ^ far) for i_2 in range(devices)])  8.93 us
    rev x2, local copies, waits for them, and re-layouts, on_device(): antipodal[:, :, 5:2:-1]  7.47 us
  transfers between devices with their start and end apart: 14, of which 10 were waited for; matrix products, arithmetic and copies ran while one was open for 10% of the time, Pallas kernels for 0%

profile of v1, /device:TPU:0, one launch (start us, length us, event | category | flops | bytes accessed | tf_op | source)
XLA Modules:
  0.0 267.6 jit_solution(14268148471364191440)
XLA Ops:
  0.0 1.3 fusion.128
  1.3 0.9 pad_maximum_fusion.28
  2.2 4.1 %collective-permute-start.4 = (f32[5,4,6,720]{3,2,1,0:T(8,128)}, f32[5,4,6,720]{3,2,1,0:T(8,128)}, u32[]{:S(2)}, u32[]{:S(2)}) collective-permute-start(f32[5,4,6,720]{3,2,1,0:T(8,128)} %pad_maximum_fusion.28), channel_id=1, source_target_pairs={{0,2},{1,3},{2,0},{3,1},{4,6},{5,7},{6,4},{7,5},{8,10},{9,11},{10,... | collective-permute-start | bytes 1036808 | tf_op jit(solution)/shard_map/ppermute | solution.py:29
  6.3 1.0 pad_maximum_fusion.25
  7.3 0.9 fusion.124
  8.2 2.6 collective-permute-start.1
  11.0 10.8 %fusion.5 = (f32[720,720]{1,0:T(8,128)S(1)}, f32[720,720]{1,0:T(8,128)}) fusion(s32[720]{0:T(1024)S(1)} %iota_add_fusion), kind=kLoop, calls=%fused_computation.8 | loop fusion | flops 4665600 | bytes 4150080 | tf_op jit(solution)/shard_map/cos | solution.py:64
  21.8 1.4 fusion.12
  23.3 1.6 collective-permute-start.2
  25.0 2.2 collective-permute-start.3
  27.3 0.8 abs_multiply_fusion.1
  28.1 5.6 %collective-permute-done.2 = f32[28,14,3]{2,1,0:T(8,128)S(1)} collective-permute-done((f32[28,14,3]{2,1,0:T(8,128)S(1)}, f32[28,14,3]{2,1,0:T(8,128)S(1)}, u32[]{:S(2)}, u32[]{:S(2)}) %collective-permute-start.2) | collective-permute-done | bytes 4736 | tf_op jit(solution)/shard_map/ppermute | solution.py:18
  33.7 4.4 %collective-permute-done.3 = f32[28,14,3]{2,1,0:T(8,128)S(1)} collective-permute-done((f32[28,14,3]{2,1,0:T(8,128)S(1)}, f32[28,14,3]{2,1,0:T(8,128)S(1)}, u32[]{:S(2)}, u32[]{:S(2)}) %collective-permute-start.3) | collective-permute-done | bytes 4736 | tf_op jit(solution)/shard_map/ppermute | solution.py:20
  38.1 1.7 fusion.60
  39.8 0.4 fusion.107
  40.3 0.9 broadcast_compare_fusion.3
  41.2 1.0 slice.329
  42.2 1.4 fusion.100
  43.6 2.1 fusion.127
  45.6 3.7 %rev.12 = f32[5,4,3,720]{3,2,1,0:T(4,128)} reverse(f32[5,4,3,720]{3,2,1,0:T(4,128)} %get-tuple-element.29), dimensions={2} | reverse | bytes 345600 | tf_op jit(solution)/shard_map/rev | solution.py:107
  49.4 3.7 %rev.13 = f32[5,4,3,720]{3,2,1,0:T(4,128)} reverse(f32[5,4,3,720]{3,2,1,0:T(4,128)} %get-tuple-element.30), dimensions={2} | reverse | bytes 345600 | tf_op jit(solution)/shard_map/rev | solution.py:111
  53.1 1.3 slice_select_fusion.3
  54.5 1.2 pad_maximum_fusion.21
  55.7 0.4 fusion.56
  56.2 0.5 copy-done.19
  56.8 1.0 fusion.43
  58.0 0.2 fusion.93
  58.2 1.4 copy-done
  59.6 3.3 %fusion.10 = f32[160,1440]{1,0:T(8,128)S(1)} fusion(f32[160,720]{1,0:T(8,128)S(1)} %bitcast.30, f32[720,720]{1,0:T(8,128)S(1)} %copy-done, f32[720,720]{1,0:T(8,128)S(1)} %get-tuple-element.41), kind=kOutput, calls=%fused_computation.13 | convolution fusion | flops 1991692800 | bytes 5529600 | tf_op jit(solution)/shard_map/dot_general | solution.py:128
  62.9 0.8 collective-permute-start.5
  63.7 21.9 %collective-permute-done.5 = f32[160,1440]{1,0:T(8,128)S(1)} collective-permute-done((f32[160,1440]{1,0:T(8,128)S(1)}, f32[160,1440]{1,0:T(8,128)S(1)}, u32[]{:S(2)}, u32[]{:S(2)}) %collective-permute-start.5) | collective-permute-done | bytes 921632 | tf_op jit(solution)/shard_map/ppermute | solution.py:132
  85.6 1.1 add.172
  86.7 2.7 %collective-permute-start.6 = (f32[160,1440]{1,0:T(8,128)}, f32[160,1440]{1,0:T(8,128)}, u32[]{:S(2)}, u32[]{:S(2)}) collective-permute-start(f32[160,1440]{1,0:T(8,128)} %add.172), channel_id=1, source_target_pairs={{0,2},{1,3},{2,0},{3,1},{4,6},{5,7},{6,4},{7,5},{8,10},{9,11},{10,... | collective-permute-start | bytes 2764808 | tf_op jit(solution)/shard_map/ppermute | solution.py:132
  89.9 41.0 %collective-permute-done.6 = f32[160,1440]{1,0:T(8,128)} collective-permute-done((f32[160,1440]{1,0:T(8,128)}, f32[160,1440]{1,0:T(8,128)}, u32[]{:S(2)}, u32[]{:S(2)}) %collective-permute-start.6) | collective-permute-done | bytes 921632 | tf_op jit(solution)/shard_map/ppermute | solution.py:132
  130.9 6.8 %fusion.15 = f32[160,720]{1,0:T(8,128)S(1)} fusion(f32[160,720]{1,0:T(8,128)S(1)} %bitcast.31, f32[720,720]{1,0:T(8,128)} %get-tuple-element.42, f32[720,720]{1,0:T(8,128)S(1)} %get-tuple-element.41, f32[160,720]{1,0:T(8,128)S(1)} %fusion.109, f32[160,1440]{1,0:T(8,128)} %add.172, f32[160,1440]{1,0:T(8,128)} %collective-permute-done.6, ...), kind=kOutput, calls=%fused_computation.34 | convolution fusion | flops 1992499200 | bytes 7372960 | tf_op jit(solution)/shard_map/dot_general | solution.py:137
  138.0 4.2 %collective-permute-start.8 = (f32[28,3,720]{2,1,0:T(4,128)S(1)}, f32[28,3,720]{2,1,0:T(4,128)S(1)}, u32[]{:S(2)}, u32[]{:S(2)}) collective-permute-start(f32[28,3,720]{2,1,0:T(4,128)S(1)} %get-tuple-element.22), channel_id=1, source_target_pairs={{4,0},{8,4},{12,8},{16,12},{20,16},{24,20},{28,24},{0,28},{5,1},{9... | collective-permute-start | bytes 725768 | tf_op jit(solution)/shard_map/ppermute | solution.py:20
  142.5 5.1 %collective-permute-done.7 = f32[28,3,720]{2,1,0:T(4,128)S(1)} collective-permute-done((f32[28,3,720]{2,1,0:T(4,128)S(1)}, f32[28,3,720]{2,1,0:T(4,128)S(1)}, u32[]{:S(2)}, u32[]{:S(2)}) %collective-permute-start.7) | collective-permute-done | bytes 241952 | tf_op jit(solution)/shard_map/ppermute | solution.py:18
  147.6 0.7 collective-permute-done.8
  148.3 0.3 fusion.14
  148.7 1.4 collective-permute-start.9
  150.1 3.1 %collective-permute-start.10 = (f32[28,14,3]{2,1,0:T(8,128)S(1)}, f32[28,14,3]{2,1,0:T(8,128)S(1)}, u32[]{:S(2)}, u32[]{:S(2)}) collective-permute-start(f32[28,14,3]{2,1,0:T(8,128)S(1)} %get-tuple-element.14), channel_id=1, source_target_pairs={{1,0},{2,1},{3,2},{0,3},{5,4},{6,5},{7,6},{4,7},{9,8},{10,9},{11,1... | collective-permute-start | bytes 14120 | tf_op jit(solution)/shard_map/ppermute | solution.py:20
  153.3 0.8 abs_multiply_fusion
  154.1 7.5 %collective-permute-done.9 = f32[28,14,3]{2,1,0:T(8,128)S(1)} collective-permute-done((f32[28,14,3]{2,1,0:T(8,128)S(1)}, f32[28,14,3]{2,1,0:T(8,128)S(1)}, u32[]{:S(2)}, u32[]{:S(2)}) %collective-permute-start.9) | collective-permute-done | bytes 4736 | tf_op jit(solution)/shard_map/ppermute | solution.py:18
  161.6 11.3 %collective-permute-done.10 = f32[28,14,3]{2,1,0:T(8,128)S(1)} collective-permute-done((f32[28,14,3]{2,1,0:T(8,128)S(1)}, f32[28,14,3]{2,1,0:T(8,128)S(1)}, u32[]{:S(2)}, u32[]{:S(2)}) %collective-permute-start.10) | collective-permute-done | bytes 4736 | tf_op jit(solution)/shard_map/ppermute | solution.py:20
  172.9 0.7 fusion.64
  173.6 0.4 fusion.89
  174.2 1.0 slice.362
  175.2 1.4 fusion.82
  176.5 0.9 fusion.125
  177.4 3.7 %rev.14 = f32[5,4,3,720]{3,2,1,0:T(4,128)} reverse(f32[5,4,3,720]{3,2,1,0:T(4,128)} %get-tuple-element.25), dimensions={2} | reverse | bytes 345600 | tf_op jit(solution)/shard_map/rev | solution.py:107
  181.2 3.7 %rev.15 = f32[5,4,3,720]{3,2,1,0:T(4,128)} reverse(f32[5,4,3,720]{3,2,1,0:T(4,128)} %get-tuple-element.26), dimensions={2} | reverse | bytes 345600 | tf_op jit(solution)/shard_map/rev | solution.py:111
  184.9 1.6 slice_select_fusion.1
  186.5 0.2 pad_maximum_fusion.23
  186.8 0.4 fusion.53
  187.2 0.5 copy-done.17
  187.8 1.0 fusion.26
  188.9 0.2 fusion.75
  189.1 1.4 copy-done.1
  190.5 3.2 %fusion.8 = f32[160,1440]{1,0:T(8,128)S(1)} fusion(f32[160,720]{1,0:T(8,128)S(1)} %bitcast.32, f32[720,720]{1,0:T(8,128)S(1)} %copy-done.1, f32[720,720]{1,0:T(8,128)S(1)} %get-tuple-element.41), kind=kOutput, calls=%fused_computation.11 | convolution fusion | flops 1991692800 | bytes 5529600 | tf_op jit(solution)/shard_map/dot_general | solution.py:128
  193.7 3.0 %collective-permute-start.12 = (f32[160,1440]{1,0:T(8,128)S(1)}, f32[160,1440]{1,0:T(8,128)S(1)}, u32[]{:S(2)}, u32[]{:S(2)}) collective-permute-start(f32[160,1440]{1,0:T(8,128)S(1)} %fusion.8), channel_id=1, source_target_pairs={{0,1},{1,0},{2,3},{3,2},{4,5},{5,4},{6,7},{7,6},{8,9},{9,8},{10,11... | collective-permute-start | bytes 2764808 | tf_op jit(solution)/shard_map/ppermute | solution.py:132
  196.7 20.9 %collective-permute-done.12 = f32[160,1440]{1,0:T(8,128)S(1)} collective-permute-done((f32[160,1440]{1,0:T(8,128)S(1)}, f32[160,1440]{1,0:T(8,128)S(1)}, u32[]{:S(2)}, u32[]{:S(2)}) %collective-permute-start.12) | collective-permute-done | bytes 921632 | tf_op jit(solution)/shard_map/ppermute | solution.py:132
  217.8 2.4 collective-permute-start.13
  220.2 42.0 %collective-permute-done.13 = f32[160,1440]{1,0:T(8,128)S(1)} collective-permute-done((f32[160,1440]{1,0:T(8,128)S(1)}, f32[160,1440]{1,0:T(8,128)S(1)}, u32[]{:S(2)}, u32[]{:S(2)}) %collective-permute-start.13) | collective-permute-done | bytes 921632 | tf_op jit(solution)/shard_map/ppermute | solution.py:132
  262.2 5.4 %fusion.16 = f32[160,720]{1,0:T(8,128)} fusion(f32[160,720]{1,0:T(8,128)S(1)} %bitcast.33, f32[720,720]{1,0:T(8,128)S(1)} %copy-done.1, f32[720,720]{1,0:T(8,128)S(1)} %get-tuple-element.41, f32[160,720]{1,0:T(8,128)S(1)} %copy-done.15, f32[160,1440]{1,0:T(8,128)S(1)} %add.188, f32[160,1440]{1,0:T(8,128)S(1)} %collective-permute-done.13, ...), kind=kOutput, calls=%fused_computation.35 | convolution fusion | flops 1992499200 | bytes 7372960 | tf_op jit(solution)/shard_map/dot_general | solution.py:137
  (76 shorter events, 2.3 us)
Async XLA Ops:
  0.0 6.3 %copy-start.3 = (f32[5,4,8,720]{3,2,1,0:T(8,128)S(1)}, f32[5,4,8,720]{3,2,1,0:T(8,128)}, u32[]{:S(2)}) copy-start(f32[5,4,8,720]{3,2,1,0:T(8,128)} %param.4) | copy-start | bytes 1382404
  2.2 41.4 %collective-permute-start.4 = (f32[5,4,6,720]{3,2,1,0:T(8,128)}, f32[5,4,6,720]{3,2,1,0:T(8,128)}, u32[]{:S(2)}, u32[]{:S(2)}) collective-permute-start(f32[5,4,6,720]{3,2,1,0:T(8,128)} %pad_maximum_fusion.28), channel_id=1, source_target_pairs={{0,2},{1,3},{2,0},{3,1},{4,6},{5,7},{6,4},{7,5},{8,10},{9,11},{10,... | collective-permute-start | bytes 1036808 | tf_op jit(solution)/shard_map/ppermute | solution.py:29
  8.2 13.6 %collective-permute-start = (f32[28,3,720]{2,1,0:T(4,128)}, f32[28,3,720]{2,1,0:T(4,128)}, u32[]{:S(2)}, u32[]{:S(2)}) collective-permute-start(f32[28,3,720]{2,1,0:T(4,128)} %get-tuple-element.23), channel_id=1, source_target_pairs={{0,4},{4,8},{8,12},{12,16},{16,20},{20,24},{24,28},{28,0},{1,5},{5... | collective-permute-start | bytes 725768 | tf_op jit(solution)/shard_map/ppermute | solution.py:18
  8.2 13.6 %collective-permute-start.1 = (f32[28,3,720]{2,1,0:T(4,128)}, f32[28,3,720]{2,1,0:T(4,128)S(1)}, u32[]{:S(2)}, u32[]{:S(2)}) collective-permute-start(f32[28,3,720]{2,1,0:T(4,128)} %get-tuple-element.24), channel_id=1, source_target_pairs={{4,0},{8,4},{12,8},{16,12},{20,16},{24,20},{28,24},{0,28},{5,1},{9... | collective-permute-start | bytes 725768 | tf_op jit(solution)/shard_map/ppermute | solution.py:20
  11.0 10.8 %copy-start.6 = (f32[4,8,720]{2,1,0:T(8,128)S(1)}, f32[4,8,720]{2,1,0:T(8,128)}, u32[]{:S(2)}) copy-start(f32[4,8,720]{2,1,0:T(8,128)} %param.6) | copy-start | bytes 276484
  11.0 10.8 %copy-start.7 = (f32[4,8,720]{2,1,0:T(8,128)S(1)}, f32[4,8,720]{2,1,0:T(8,128)}, u32[]{:S(2)}) copy-start(f32[4,8,720]{2,1,0:T(8,128)} %param.5) | copy-start | bytes 276484
  21.8 16.3 %copy-start.4 = (f32[5,4,8,720]{3,2,1,0:T(8,128)S(1)}, f32[5,4,8,720]{3,2,1,0:T(8,128)}, u32[]{:S(2)}) copy-start(f32[5,4,8,720]{3,2,1,0:T(8,128)} %param.4) | copy-start | bytes 1382404
  21.8 5.4 %copy-start.10 = (f32[28,3,720]{2,1,0:T(4,128)}, f32[28,3,720]{2,1,0:T(4,128)S(1)}, u32[]{:S(2)}) copy-start(f32[28,3,720]{2,1,0:T(4,128)S(1)} %collective-permute-done.1) | copy-start | bytes 725764
  23.3 10.4 %collective-permute-start.2 = (f32[28,14,3]{2,1,0:T(8,128)S(1)}, f32[28,14,3]{2,1,0:T(8,128)S(1)}, u32[]{:S(2)}, u32[]{:S(2)}) collective-permute-start(f32[28,14,3]{2,1,0:T(8,128)S(1)} %get-tuple-element.15), channel_id=1, source_target_pairs={{0,1},{1,2},{2,3},{3,0},{4,5},{5,6},{6,7},{7,4},{8,9},{9,10},{10,1... | collective-permute-start | bytes 14120 | tf_op jit(solution)/shard_map/ppermute | solution.py:18
  25.0 13.1 %collective-permute-start.3 = (f32[28,14,3]{2,1,0:T(8,128)S(1)}, f32[28,14,3]{2,1,0:T(8,128)S(1)}, u32[]{:S(2)}, u32[]{:S(2)}) collective-permute-start(f32[28,14,3]{2,1,0:T(8,128)S(1)} %get-tuple-element.16), channel_id=1, source_target_pairs={{1,0},{2,1},{3,2},{0,3},{5,4},{6,5},{7,6},{4,7},{9,8},{10,9},{11,1... | collective-permute-start | bytes 14120 | tf_op jit(solution)/shard_map/ppermute | solution.py:20
  27.3 6.4 %copy-start.18 = (f32[4,9,720]{2,1,0:T(8,128)}, f32[4,9,720]{2,1,0:T(8,128)S(1)}, u32[]{:S(2)}) copy-start(f32[4,9,720]{2,1,0:T(8,128)S(1)} %get-tuple-element.12) | copy-start | bytes 311044
  28.1 12.2 %copy-start.11 = (f32[28,3,720]{2,1,0:T(4,128)S(1)}, f32[28,3,720]{2,1,0:T(4,128)}, u32[]{:S(2)}) copy-start(f32[28,3,720]{2,1,0:T(4,128)} %copy-done.10) | copy-start | bytes 725764
  53.1 2.6 copy-start.9
  55.7 0.9 copy-start.19
  55.7 1.0 copy-start.22
  55.7 1.1 copy-start.23
  56.8 1.0 copy-start.5
  56.8 1.2 copy-start.13
  58.0 1.6 copy-start
  62.9 26.7 %copy-start.24 = (s32[64]{0:T(128)S(1)}, s32[64]{0:T(128)}, u32[]{:S(2)}) copy-start(s32[64]{0:T(128)} %param.7) | copy-start | bytes 772
  62.9 22.7 %collective-permute-start.5 = (f32[160,1440]{1,0:T(8,128)S(1)}, f32[160,1440]{1,0:T(8,128)S(1)}, u32[]{:S(2)}, u32[]{:S(2)}) collective-permute-start(f32[160,1440]{1,0:T(8,128)S(1)} %fusion.10), channel_id=1, source_target_pairs={{0,1},{1,0},{2,3},{3,2},{4,5},{5,4},{6,7},{7,6},{8,9},{9,8},{10,11... | collective-permute-start | bytes 2764808 | tf_op jit(solution)/shard_map/ppermute | solution.py:132
  86.7 44.2 %collective-permute-start.6 = (f32[160,1440]{1,0:T(8,128)}, f32[160,1440]{1,0:T(8,128)}, u32[]{:S(2)}, u32[]{:S(2)}) collective-permute-start(f32[160,1440]{1,0:T(8,128)} %add.172), channel_id=1, source_target_pairs={{0,2},{1,3},{2,0},{3,1},{4,6},{5,7},{6,4},{7,5},{8,10},{9,11},{10,... | collective-permute-start | bytes 2764808 | tf_op jit(solution)/shard_map/ppermute | solution.py:132
  89.9 47.9 %copy-start.14 = (f32[160,720]{1,0:T(8,128)}, f32[160,720]{1,0:T(8,128)S(1)}, u32[]{:S(2)}) copy-start(f32[160,720]{1,0:T(8,128)S(1)} %fusion.109) | copy-start | bytes 1382404
  137.9 9.7 %collective-permute-start.7 = (f32[28,3,720]{2,1,0:T(4,128)S(1)}, f32[28,3,720]{2,1,0:T(4,128)S(1)}, u32[]{:S(2)}, u32[]{:S(2)}) collective-permute-start(f32[28,3,720]{2,1,0:T(4,128)S(1)} %get-tuple-element.21), channel_id=1, source_target_pairs={{0,4},{4,8},{8,12},{12,16},{16,20},{20,24},{24,28},{28,0},{1,5},{5... | collective-permute-start | bytes 725768 | tf_op jit(solution)/shard_map/ppermute | solution.py:18
  138.0 10.3 %collective-permute-start.8 = (f32[28,3,720]{2,1,0:T(4,128)S(1)}, f32[28,3,720]{2,1,0:T(4,128)S(1)}, u32[]{:S(2)}, u32[]{:S(2)}) collective-permute-start(f32[28,3,720]{2,1,0:T(4,128)S(1)} %get-tuple-element.22), channel_id=1, source_target_pairs={{4,0},{8,4},{12,8},{16,12},{20,16},{24,20},{28,24},{0,28},{5,1},{9... | collective-permute-start | bytes 725768 | tf_op jit(solution)/shard_map/ppermute | solution.py:20
  142.4 34.1 %collective-permute-start.11 = (f32[5,4,6,720]{3,2,1,0:T(8,128)S(1)}, f32[5,4,6,720]{3,2,1,0:T(8,128)S(1)}, u32[]{:S(2)}, u32[]{:S(2)}) collective-permute-start(f32[5,4,6,720]{3,2,1,0:T(8,128)S(1)} %pad_maximum_fusion.29), channel_id=1, source_target_pairs={{0,2},{1,3},{2,0},{3,1},{4,6},{5,7},{6,4},{7,5},{8,10},{9,11},{10,... | collective-permute-start | bytes 1036808 | tf_op jit(solution)/shard_map/ppermute | solution.py:29
  148.7 12.9 %collective-permute-start.9 = (f32[28,14,3]{2,1,0:T(8,128)S(1)}, f32[28,14,3]{2,1,0:T(8,128)S(1)}, u32[]{:S(2)}, u32[]{:S(2)}) collective-permute-start(f32[28,14,3]{2,1,0:T(8,128)S(1)} %get-tuple-element.13), channel_id=1, source_target_pairs={{0,1},{1,2},{2,3},{3,0},{4,5},{5,6},{6,7},{7,4},{8,9},{9,10},{10,1... | collective-permute-start | bytes 14120 | tf_op jit(solution)/shard_map/ppermute | solution.py:18
  150.1 22.8 %collective-permute-start.10 = (f32[28,14,3]{2,1,0:T(8,128)S(1)}, f32[28,14,3]{2,1,0:T(8,128)S(1)}, u32[]{:S(2)}, u32[]{:S(2)}) collective-permute-start(f32[28,14,3]{2,1,0:T(8,128)S(1)} %get-tuple-element.14), channel_id=1, source_target_pairs={{1,0},{2,1},{3,2},{0,3},{5,4},{6,5},{7,6},{4,7},{9,8},{10,9},{11,1... | collective-permute-start | bytes 14120 | tf_op jit(solution)/shard_map/ppermute | solution.py:20
  153.3 8.4 %copy-start.16 = (f32[4,9,720]{2,1,0:T(8,128)}, f32[4,9,720]{2,1,0:T(8,128)S(1)}, u32[]{:S(2)}) copy-start(f32[4,9,720]{2,1,0:T(8,128)S(1)} %get-tuple-element.8) | copy-start | bytes 311044
  173.6 1.6 copy-start.2
  176.5 10.0 %copy-start.8 = (f32[5,4,8,720]{3,2,1,0:T(8,128)S(1)}, f32[5,4,8,720]{3,2,1,0:T(8,128)}, u32[]{:S(2)}) copy-start(f32[5,4,8,720]{3,2,1,0:T(8,128)} %slice.362) | copy-start | bytes 1382404
  186.7 0.9 copy-start.17
  186.7 1.0 copy-start.20
  186.7 1.1 copy-start.21
  187.8 1.0 copy-start.12
  188.9 1.6 copy-start.1
  193.7 68.5 %copy-start.15 = (f32[160,720]{1,0:T(8,128)S(1)}, f32[160,720]{1,0:T(8,128)}, u32[]{:S(2)}) copy-start(f32[160,720]{1,0:T(8,128)} %copy-done.14) | copy-start | bytes 1382404
  193.7 23.9 %collective-permute-start.12 = (f32[160,1440]{1,0:T(8,128)S(1)}, f32[160,1440]{1,0:T(8,128)S(1)}, u32[]{:S(2)}, u32[]{:S(2)}) collective-permute-start(f32[160,1440]{1,0:T(8,128)S(1)} %fusion.8), channel_id=1, source_target_pairs={{0,1},{1,0},{2,3},{3,2},{4,5},{5,4},{6,7},{7,6},{8,9},{9,8},{10,11... | collective-permute-start | bytes 2764808 | tf_op jit(solution)/shard_map/ppermute | solution.py:132
  217.8 44.4 %collective-permute-start.13 = (f32[160,1440]{1,0:T(8,128)S(1)}, f32[160,1440]{1,0:T(8,128)S(1)}, u32[]{:S(2)}, u32[]{:S(2)}) collective-permute-start(f32[160,1440]{1,0:T(8,128)S(1)} %add.188), channel_id=1, source_target_pairs={{0,2},{1,3},{2,0},{3,1},{4,6},{5,7},{6,4},{7,5},{8,10},{9,11},{10,... | collective-permute-start | bytes 2764808 | tf_op jit(solution)/shard_map/ppermute | solution.py:132
